TPU v7x, 128 devices: a whole 4x4x4 slice. The times are simulated.
128 devices in a mesh: req: 16 (over y, z), tp: 8 (over x, core).
Axes of the slice: x: 4, y: 4, z: 4, core: 2. Of those that a mesh axis runs over, the one named last changes fastest.
Arguments:
- suffix_tokens: bfloat16 [256, 112, 2880], P('req'), may hold values from -40 to 40
- route_lengths: int32 [16, 16], replicated, may hold values from 1 to 112, 768 in all within a row
- dest_perm: int32 [16, 16], replicated, may hold values from 0 to 15, each once within a row
- attach_points: int32 [256], replicated, may hold values from 256 to 8192
- prefix_cache: bfloat16 [64, 128, 8, 128], P('req', None, 'tp'), may hold values from -120 to 120
- block_of_slot: int32 [64], replicated, may hold values from 0 to 63, each once
- sink_logits: float32 [64], P('tp'), may hold values from 0 to 6
- attn_gain: bfloat16 [2880], replicated, may hold values from 0.099609375 to 1.8984375
- w_query: bfloat16 [2880, 4096], P(None, 'tp'), may hold values from -0.109375 to 0.109375
- w_keyval: bfloat16 [2880, 8, 128], P(None, 'tp'), may hold values from -0.109375 to 0.109375
- w_out: bfloat16 [4096, 2880], P('tp'), may hold values from -0.09375 to 0.09375
- mlp_gain: bfloat16 [2880], replicated, may hold values from 0.099609375 to 1.8984375
- w_gate: bfloat16 [2880, 2880], P(None, 'tp'), may hold values from -0.109375 to 0.109375
- w_up: bfloat16 [2880, 2880], P(None, 'tp'), may hold values from -0.109375 to 0.109375
- w_down: bfloat16 [2880, 2880], P('tp'), may hold values from -0.109375 to 0.109375
Outputs:
- layer_out: bfloat16 [256, 112, 2880], P('req', None, 'tp')
Inputs may be any that keep to these rules, and one draw needn't show every extreme that they name: `route_lengths`: each row sums to 768, and the largest entry of each row is 112. `dest_perm`: each row is a permutation of the devices of req. `block_of_slot`: a permutation.
All inputs are finite; a program needn't handle non-finite values.
Results may differ from a plain program's by a relative error of at most 0.013.
Values may be sent and summed in bfloat16 or wider, within the bound.
No kernel may reach another device: no remote copies, remote signals or barrier semaphores. Data moves between devices by JAX's collectives and lax.ppermute only.
A program may use at most 192 MiB of HBM per device.

v0:
```python
import jax
import jax.numpy as jnp
from jax import lax
from jax.sharding import PartitionSpec as P

WINDOW = 128
CAP = 768
ROPE_BASE = 150000.0
EPSILON = 1e-05


def norm_rows(inputs, gains):
    widened = inputs.astype(jnp.float32)
    factor = lax.rsqrt(jnp.mean(widened * widened, axis=-1, keepdims=True) + EPSILON)
    return (widened * factor * gains.astype(jnp.float32)).astype(jnp.bfloat16)


def rotate(vectors, positions):
    half_dim = vectors.shape[-1] // 2
    frequency = ROPE_BASE ** (-(jnp.arange(half_dim).astype(jnp.float32) * 2.0 / vectors.shape[-1]))
    angles = positions.astype(jnp.float32)[:, None, None] * frequency
    cosine = jnp.cos(angles)
    sine_part = jnp.sin(angles)
    first_half = vectors[..., :half_dim]
    second = vectors[..., half_dim:]
    return jnp.concatenate(
        [first_half * cosine - second * sine_part, second * cosine + first_half * sine_part],
        axis=-1,
    )


def attend(query_slots, paired_slots, tail_rows, sink_logits):
    peers, slot_length = (query_slots.shape[0], query_slots.shape[1])
    value_heads = paired_slots.shape[2]
    head_dim = paired_slots.shape[3] // 2
    group_size = query_slots.shape[2] // value_heads
    window = tail_rows.shape[1]
    grouped_query = query_slots.reshape(peers, slot_length, value_heads, group_size, head_dim)
    near_keys = jnp.concatenate([tail_rows, paired_slots], axis=1)
    score_scale = head_dim ** (-0.5)
    near_scores = (
        jnp.einsum(
            "ntkgd,nskd->nkgts",
            grouped_query,
            near_keys[..., :head_dim],
            preferred_element_type=jnp.float32,
        )
        * score_scale
    )
    sink_scores = sink_logits.reshape(value_heads, group_size)[None, :, :, None, None]
    slot_steps = jnp.arange(slot_length)
    columns = jnp.arange(window + slot_length)
    allowed = jnp.where(
        columns[None, :] < window,
        columns[None, :] > slot_steps[:, None],
        columns[None, :] - window <= slot_steps[:, None],
    )
    near_scores = jnp.where(allowed, near_scores, -jnp.inf)
    largest = jnp.maximum(jnp.max(near_scores, axis=-1, keepdims=True), sink_scores)
    near_weights = jnp.exp(near_scores - largest)
    normalizer = jnp.sum(near_weights, axis=-1, keepdims=True) + jnp.exp(sink_scores - largest)
    near_weights = (near_weights / normalizer).astype(jnp.bfloat16)
    mixed = jnp.einsum(
        "nkgts,nskd->ntkgd",
        near_weights,
        near_keys[..., head_dim:],
        preferred_element_type=jnp.float32,
    )
    return mixed.astype(jnp.bfloat16).reshape(
        peers * slot_length, value_heads * group_size * head_dim
    )


def fetch_prefix(attach_slots, prefix_cache, block_of_slot, window):
    total_blocks = block_of_slot.shape[0]
    block_len = prefix_cache.shape[1]
    catalog = jnp.arange(total_blocks)
    home_row = jnp.sum(
        jnp.where(block_of_slot[None, :] == catalog[:, None], catalog[None, :], 0), axis=1
    )
    wanted = attach_slots[:, None] - window + jnp.arange(window)[None, :]
    block_id = wanted // block_len
    tail_store = jnp.sum(jnp.where(block_id[..., None] == catalog, home_row, 0), axis=-1)
    tail_offset = wanted - block_id * block_len
    trailing = prefix_cache.shape[2:]
    initial = jnp.zeros((attach_slots.shape[0], window) + trailing, jnp.bfloat16)
    shard_rows = lax.all_gather(prefix_cache, "req", axis=0, tiled=True)
    held_blocks = shard_rows.shape[0]
    flat_rows = shard_rows.reshape((held_blocks * block_len,) + trailing)
    inside = (tail_store >= 0) & (tail_store < held_blocks)
    picked = flat_rows[jnp.clip(tail_store, 0, held_blocks - 1) * block_len + tail_offset]
    return jnp.where(inside[..., None, None], picked, initial)


def local(
    suffix_tokens,
    route_lengths,
    dest_perm,
    attach_points,
    prefix_cache,
    block_of_slot,
    sink_logits,
    attn_gain,
    w_query,
    w_keyval,
    w_out,
    mlp_gain,
    w_gate,
    w_up,
    w_down,
):
    peers = lax.axis_size("req")
    splits = lax.axis_size("tp")
    request_index = lax.axis_index("req")
    tensor_index = lax.axis_index("tp")
    slot_count, slot_length, features = suffix_tokens.shape
    feature_share = features // splits
    value_heads = w_keyval.shape[1]
    head_dim = w_keyval.shape[2] // 2
    peer_ids = jnp.arange(peers)
    slot_steps = jnp.arange(slot_length)
    my_row = lax.dynamic_index_in_dim(dest_perm, request_index, 0, keepdims=False)
    attach_table = attach_points.reshape(peers, peers)
    arriving_lengths = lax.dynamic_index_in_dim(route_lengths, request_index, 0, keepdims=False)
    arriving = (dest_perm == request_index).astype(jnp.int32)
    arriving_attach = jnp.sum(attach_table * arriving, axis=1)
    send_order = jnp.sum(
        jnp.where(my_row[None, :] == peer_ids[:, None], peer_ids[None, :], 0), axis=1
    )
    run_ends = jnp.cumsum(arriving_lengths)
    starts = run_ends - arriving_lengths
    packed_ids = jnp.arange(CAP)
    source_of = jnp.sum((run_ends[None, :] <= packed_ids[:, None]).astype(jnp.int32), axis=1)
    source_hot = (source_of[:, None] == peer_ids[None, :]).astype(jnp.int32)
    token_index = packed_ids - jnp.sum(source_hot * starts[None, :], axis=1)
    positions = jnp.sum(source_hot * arriving_attach[None, :], axis=1) + token_index
    flat_index = source_of * slot_length + token_index
    slot_source = jnp.clip(starts[:, None] + slot_steps[None, :], 0, CAP - 1).reshape(-1)
    live_mask = slot_steps[None, :] < arriving_lengths[:, None]

    def to_slots(values):
        return values[slot_source].reshape((peers, slot_length) + values.shape[1:])

    tail_rows = fetch_prefix(arriving_attach, prefix_cache, block_of_slot, WINDOW)
    landed = lax.all_to_all(
        suffix_tokens[send_order], "req", split_axis=0, concat_axis=0, tiled=True
    )
    input_rows = landed.reshape(peers * slot_length, features)[flat_index]
    row_total = input_rows.shape[0]
    normed_in = norm_rows(input_rows, attn_gain)
    queries = jnp.dot(normed_in, w_query, preferred_element_type=jnp.float32).reshape(
        row_total, -1, head_dim
    )
    queries = rotate(queries, positions).astype(jnp.bfloat16)
    paired = jnp.dot(
        normed_in, w_keyval.reshape(features, -1), preferred_element_type=jnp.float32
    ).reshape(row_total, value_heads, 2 * head_dim)
    rotated = rotate(paired[..., :head_dim], positions)
    paired = jnp.concatenate([rotated, paired[..., head_dim:]], axis=-1).astype(jnp.bfloat16)
    attended = attend(to_slots(queries), to_slots(paired), tail_rows, sink_logits)[flat_index]
    partial_value = jnp.dot(attended, w_out, preferred_element_type=jnp.float32)
    summed = lax.psum(partial_value.astype(jnp.bfloat16), "tp").astype(jnp.float32)
    residual = (input_rows.astype(jnp.float32) + summed).astype(jnp.bfloat16)
    normed_mid = norm_rows(residual, mlp_gain)
    residual_part = lax.dynamic_slice_in_dim(
        residual, tensor_index * feature_share, feature_share, 1
    )
    gate_proj = jnp.dot(normed_mid, w_gate, preferred_element_type=jnp.float32)
    up_proj = jnp.dot(normed_mid, w_up, preferred_element_type=jnp.float32)
    hidden = (jax.nn.silu(gate_proj) * up_proj).astype(jnp.bfloat16)
    down_sum = lax.psum_scatter(
        jnp.dot(hidden, w_down, preferred_element_type=jnp.float32).astype(jnp.bfloat16),
        "tp",
        scatter_dimension=1,
        tiled=True,
    ).astype(jnp.float32)
    out_rows = (residual_part.astype(jnp.float32) + down_sum).astype(jnp.bfloat16)
    out_slots = jnp.where(live_mask[..., None], to_slots(out_rows), jnp.zeros((), jnp.bfloat16))
    returned = lax.all_to_all(out_slots, "req", split_axis=0, concat_axis=0, tiled=True)
    return returned[my_row]


def solution(mesh):
    in_specs = (
        P("req", None, None),
        P(),
        P(),
        P(),
        P("req", None, "tp", None),
        P(),
        P("tp"),
        P(),
        P(None, "tp"),
        P(None, "tp", None),
        P("tp", None),
        P(),
        P(None, "tp"),
        P(None, "tp"),
        P("tp", None),
    )
    out_specs = P("req", None, "tp")
    return jax.shard_map(local, mesh=mesh, in_specs=in_specs, out_specs=out_specs, check_vma=False)
```

profile of v0, /device:TPU:7, one launch (start us, length us, event | category | flops | bytes accessed | tf_op | source)
XLA Modules:
  0.0 531.0 jit_solution(8293416445364604269)
XLA Ops:
  7.5 9.7 %gather_fusion = bf16[16,112,2880]{2,1,0:T(8,128)(2,1)} fusion(bf16[16,112,2880]{2,1,0:T(8,128)(2,1)} %param.15, s32[1024]{0:T(1024)S(1)} %pad_clamp_fusion.3), kind=kCustom, calls=%fused_computation | custom fusion | bytes 20643904 | tf_op jit(solution)/shard_map/gather | solution.py:146
  17.2 8.0 %all-to-all-start = ((bf16[16,112,2880]{2,1,0:T(8,128)(2,1)}), bf16[16,112,2880]{2,1,0:T(8,128)(2,1)}, u32[]{:S(2)}, u32[]{:S(2)}) async-start(bf16[16,112,2880]{2,1,0:T(8,128)(2,1)} %gather_fusion), calls=%async_computation | async-start | bytes 21102592 | tf_op jit(solution)/shard_map/all_to_all | solution.py:145
  29.5 2.5 multiply_cosine_fusion
  32.0 176.3 %all-gather.2.cloned.1.call-done = bf16[64,128,1,128]{3,1,2,0:T(8,128)(2,1)} async-done(((bf16[4,128,1,128]{3,1,2,0:T(8,128)(2,1)}), bf16[64,128,1,128]{3,1,2,0:T(8,128)(2,1)}) %all-gather.2.cloned.1.call-update) | async-done | bytes 2097168 | tf_op jit(solution)/shard_map/all_gather | solution.py:87
  208.3 7.4 %gather_fusion.2 = bf16[2048,128]{1,0:T(8,128)(2,1)S(1)} fusion(bf16[8192,128]{1,0:T(8,128)(2,1)} %bitcast.90, s32[2048]{0:T(1024)S(1)} %fusion.52), kind=kCustom, calls=%fused_computation.2 | custom fusion | bytes 1056768 | tf_op jit(solution)/shard_map/gather | solution.py:91
  218.7 14.6 %gather_fusion.1 = bf16[768,2880]{1,0:T(8,128)(2,1)} fusion(bf16[1792,2880]{1,0:T(8,128)(2,1)} %bitcast.4, s32[1024]{0:T(1024)S(1)} %pad_clamp_fusion.2), kind=kCustom, calls=%fused_computation.1 | custom fusion | bytes 8850432 | tf_op jit(solution)/shard_map/gather | solution.py:148
  233.3 6.6 %copy.45 = bf16[768,2880]{0,1:T(8,128)(2,1)} copy(bf16[768,2880]{1,0:T(8,128)(2,1)} %gather_fusion.1) | data formatting | bytes 8847360 | tf_op jit(solution)/shard_map/gather | solution.py:148
  239.9 3.3 fusion.5
  243.5 2.6 fusion.24
  246.8 16.1 %gather_fusion.3 = bf16[1792,128]{1,0:T(8,128)(2,1)} fusion(bf16[768,128]{1,0:T(8,128)(2,1)S(1)} %copy.47, s32[2048]{0:T(1024)S(1)} %pad_clamp_fusion), kind=kCustom, calls=%fused_computation.3 | custom fusion | bytes 924672 | tf_op jit(solution)/shard_map/gather | solution.py:142
  264.9 6.1 %fusion.20 = f32[768,512]{0,1:T(8,128)S(1)} fusion(bf16[2880,512]{1,0:T(8,128)(2,1)} %param.23, bf16[768,2880]{0,1:T(8,128)(2,1)} %copy.45, f32[2880]{0:T(1024)S(1)} %convert_element_type.90, f32[768]{0:T(1024)S(1)} %add_rsqrt_fusion.1), kind=kOutput, calls=%fused_computation.40 | convolution fusion | flops 2273771520 | bytes 8960256 | tf_op jit(solution)/shard_map/dot_general | solution.py:151
  272.2 3.2 copy.62
  275.4 3.2 copy.63
  278.6 3.7 subtract_convert_fusion
  284.4 5.7 %gather_fusion.4 = bf16[1792,8,64]{2,1,0:T(8,128)(2,1)} fusion(bf16[768,8,64]{2,1,0:T(8,128)(2,1)} %pad_maximum_fusion, s32[2048]{0:T(1024)S(1)} %pad_clamp_fusion), kind=kCustom, calls=%fused_computation.4 | custom fusion | bytes 3677184 | tf_op jit(solution)/shard_map/gather | solution.py:142
  290.1 5.1 fusion.1
  295.4 5.3 fusion
  300.7 6.6 %convert_bitcast_fusion = bf16[16,112,1,8,64]{1,4,3,0,2:T(8,128)(2,1)} fusion(f32[16,8,112]{2,1,0:T(8,128)S(1)} %exponential_add_fusion, f32[16,8,112]{2,1,0:T(8,128)S(1)} %broadcast_maximum_fusion, f32[16,240,112,8]{1,2,3,0:T(8,128)S(1)} %get-tuple-element.18, pred[112,240]{1,0:T(8,128)(4,1)S(1)} %fusion.41, bf16[16,128,1,128]{1,3,0,2:T(8,128)(2,1)S(1)} %copy-done.3, ...), kind=kOutput, calls=%fused_computation.34 | convolution fusion | flops 459505664 | bytes 16722176 | tf_op jit(solution)/shard_map/nkgts,nskd->ntkgd/dot_general | solution.py:63
  307.3 4.8 copy.60
  312.2 5.9 %reshape.650 = bf16[1792,512]{1,0:T(8,128)(2,1)} reshape(bf16[16,112,1,8,64]{4,3,1,0,2:T(8,128)(2,1)} %copy.60) | data formatting | bytes 3670016 | tf_op jit(solution)/shard_map/reshape | solution.py:69
  318.1 5.1 gather_fusion.5
  323.2 5.7 %convolution_convert_fusion = bf16[768,2880]{0,1:T(8,128)(2,1)} fusion(bf16[768,512]{1,0:T(8,128)(2,1)} %gather_fusion.5, bf16[512,2880]{0,1:T(8,128)(2,1)S(1)} %copy-done), kind=kOutput, calls=%fused_computation.28 | convolution fusion | flops 2267136000 | bytes 8159232 | tf_op jit(solution)/shard_map/dot_general | solution.py:161
  329.6 91.0 %all-reduce.2.cloned.1.call-done = bf16[768,2880]{0,1:T(8,128)(2,1)} async-done(((bf16[768,2880]{0,1:T(8,128)(2,1)}), bf16[768,2880]{0,1:T(8,128)(2,1)}) %all-reduce.2.cloned.1.call-update) | async-done | bytes 4423696 | tf_op jit(solution)/shard_map/psum | solution.py:162
  420.6 5.5 %fusion.2 = (f32[768]{0:T(1024)S(1)}, bf16[768,2880]{0,1:T(8,128)(2,1)S(1)}) fusion(bf16[768,2880]{0,1:T(8,128)(2,1)} %all-reduce.2.cloned.1.call-done, bf16[768,2880]{0,1:T(8,128)(2,1)} %copy.45), kind=kLoop, calls=%fused_computation.18 | loop fusion | flops 15482112 | bytes 13274112 | tf_op jit(solution)/shard_map/reduce_sum | solution.py:14
  428.1 3.2 fusion.18
  431.4 11.4 %convolution_convert_fusion.1 = bf16[768,2880]{0,1:T(8,128)(2,1)} fusion(bf16[360,2880]{1,0:T(8,128)(2,1)} %param.29, bf16[2880,360]{0,1:T(8,128)(2,1)} %param.28, bf16[768,2880]{0,1:T(8,128)(2,1)} %copy-done.2, f32[2880]{0:T(1024)S(1)} %convert_element_type.103, f32[768]{0:T(1024)S(1)} %add_rsqrt_fusion, f32[768,360]{0,1:T(8,128)} %fusion.18), kind=kOutput, calls=%fused_computation.29 | convolution fusion | flops 3197767680 | bytes 14115072 | tf_op jit(solution)/shard_map/dot_general | solution.py:172
  443.5 36.8 %reduce-scatter.2.cloned.1.call-done = bf16[768,360]{0,1:T(8,128)(2,1)} async-done(((bf16[768,2880]{0,1:T(8,128)(2,1)}), bf16[768,360]{0,1:T(8,128)(2,1)}) %reduce-scatter.2.cloned.1.call-update) | async-done | bytes 552976 | tf_op jit(solution)/shard_map/reduce_scatter | solution.py:171
  483.9 6.0 %gather_fusion.6 = bf16[1792,360]{1,0:T(8,128)(2,1)} fusion(bf16[768,360]{1,0:T(8,128)(2,1)S(1)} %copy.55, s32[2048]{0:T(1024)S(1)} %pad_clamp_fusion), kind=kCustom, calls=%fused_computation.6 | custom fusion | bytes 2587648 | tf_op jit(solution)/shard_map/gather | solution.py:142
  489.8 2.7 broadcast_select_fusion
  492.6 6.8 %all-to-all-start.1 = ((bf16[16,112,360]{2,1,0:T(8,128)(2,1)}), bf16[16,112,360]{2,1,0:T(8,128)(2,1)}, u32[]{:S(2)}, u32[]{:S(2)}) async-start(bf16[16,112,360]{2,1,0:T(8,128)(2,1)} %broadcast_select_fusion), calls=%async_computation.2 | async-start | bytes 2752512 | tf_op jit(solution)/shard_map/all_to_all | solution.py:179
  500.1 20.9 %all-to-all-done.1 = bf16[16,112,360]{2,1,0:T(8,128)(2,1)} async-done(((bf16[16,112,360]{2,1,0:T(8,128)(2,1)}), bf16[16,112,360]{2,1,0:T(8,128)(2,1)}, u32[]{:S(2)}, u32[]{:S(2)}) %all-to-all-start.1) | async-done | bytes 1290272 | tf_op jit(solution)/shard_map/all_to_all | solution.py:179
  521.0 3.2 gather_fusion.7
  (86 shorter events, 22.2 us)
Async XLA Ops:
  6.5 316.6 %copy-start = (bf16[512,2880]{0,1:T(8,128)(2,1)S(1)}, bf16[512,2880]{0,1:T(8,128)(2,1)}, u32[]{:S(2)}) copy-start(bf16[512,2880]{0,1:T(8,128)(2,1)} %param.25) | copy-start | bytes 8847364
  17.2 9.7 %copy-start.10 = (s32[256]{0:T(256)S(1)}, s32[256]{0:T(256)}, u32[]{:S(2)}) copy-start(s32[256]{0:T(256)} %param.18) | copy-start | bytes 3076
  17.2 9.8 %copy-start.7 = (bf16[2880]{0:T(1024)(128)(2,1)S(1)}, bf16[2880]{0:T(1024)(128)(2,1)}, u32[]{:S(2)}) copy-start(bf16[2880]{0:T(1024)(128)(2,1)} %param.22) | copy-start | bytes 17284
  17.2 10.7 %copy-start.6 = (s32[16,16]{1,0:T(8,128)S(1)}, s32[16,16]{1,0:T(8,128)}, u32[]{:S(2)}) copy-start(s32[16,16]{1,0:T(8,128)} %param.17) | copy-start | bytes 3076
  17.2 11.8 %copy-start.12 = (s32[64]{0:T(128)S(1)}, s32[64]{0:T(128)}, u32[]{:S(2)}) copy-start(s32[64]{0:T(128)} %param.20) | copy-start | bytes 772
  17.2 201.5 %all-to-all-start = ((bf16[16,112,2880]{2,1,0:T(8,128)(2,1)}), bf16[16,112,2880]{2,1,0:T(8,128)(2,1)}, u32[]{:S(2)}, u32[]{:S(2)}) async-start(bf16[16,112,2880]{2,1,0:T(8,128)(2,1)} %gather_fusion), calls=%async_computation | async-start | bytes 21102592 | tf_op jit(solution)/shard_map/all_to_all | solution.py:145
  25.2 183.2 %all-gather.2.cloned.1.call-start = ((), (), s32[]{:S(2)}) async-start(), calls=%async_computation.3 | async-start | bytes 2228224 | tf_op jit(solution)/shard_map/all_gather | solution.py:87
  25.9 394.7 %all-reduce.2.cloned.1.call-start = ((), (), s32[]{:S(2)}) async-start(), calls=%async_computation.4 | async-start | bytes 8847360 | tf_op jit(solution)/shard_map/psum | solution.py:162
  239.9 3.6 copy-start.1
  272.2 6.4 %copy-start.5 = (f32[768,32]{1,0:T(8,128)S(1)}, f32[768,32]{1,0:T(8,128)}, u32[]{:S(2)}) copy-start(f32[768,32]{1,0:T(8,128)} %get-tuple-element.15) | copy-start | bytes 294916
  284.4 5.7 %copy-start.3 = (bf16[16,128,1,128]{1,3,0,2:T(8,128)(2,1)S(1)}, bf16[16,128,1,128]{1,3,0,2:T(8,128)(2,1)}, u32[]{:S(2)}) copy-start(bf16[16,128,1,128]{1,3,0,2:T(8,128)(2,1)} %broadcast_select_fusion.1) | copy-start | bytes 1572868
  290.1 5.1 copy-start.9
  295.4 5.4 %copy-start.4 = (bf16[16,112,1,128]{1,3,0,2:T(8,128)(2,1)S(1)}, bf16[16,112,1,128]{1,3,0,2:T(8,128)(2,1)}, u32[]{:S(2)}) copy-start(bf16[16,112,1,128]{1,3,0,2:T(8,128)(2,1)} %copy.48) | copy-start | bytes 1376260
  328.9 0.7 copy-start.8
  328.9 151.4 %reduce-scatter.2.cloned.1.call-start = ((), (), s32[]{:S(2)}) async-start(), calls=%async_computation.5 | async-start | bytes 4976640 | tf_op jit(solution)/shard_map/reduce_scatter | solution.py:171
  420.6 7.5 %copy-start.11 = (bf16[2880,360]{0,1:T(8,128)(2,1)S(1)}, bf16[2880,360]{0,1:T(8,128)(2,1)}, u32[]{:S(2)}) copy-start(bf16[2880,360]{0,1:T(8,128)(2,1)} %param.27) | copy-start | bytes 6220804
  426.1 2.0 copy-start.2
  492.6 28.4 %all-to-all-start.1 = ((bf16[16,112,360]{2,1,0:T(8,128)(2,1)}), bf16[16,112,360]{2,1,0:T(8,128)(2,1)}, u32[]{:S(2)}, u32[]{:S(2)}) async-start(bf16[16,112,360]{2,1,0:T(8,128)(2,1)} %broadcast_select_fusion), calls=%async_computation.2 | async-start | bytes 2752512 | tf_op jit(solution)/shard_map/all_to_all | solution.py:179
Sparse Core Ops, SparseCore 0:
  28.1 180.1 all-gather.1
  329.0 91.5 all-reduce.1
  442.9 37.4 reduce-scatter.1
where the time goes:
time: 540 us; the launch traced here: 531 us
  waiting for transfers between devices  326 us (60%)
  local copies, waits for them, and re-layouts  103 us (19%)
  matrix products  40.7 us (8%)
  other arithmetic  33.2 us (6%)
  starting transfers between devices  15 us (3%)
  between operations  13.8 us (3%)
    all_gather x1, waiting for transfers between devices, fetch_prefix(): shard_rows = lax.all_gather(prefix_cache, 'req', axis=0, tiled=True)  176 us
    psum x1, waiting for transfers between devices, local(): lax.psum(partial_value.astype(jnp.bfloat16), 'tp').astype(jnp.float32)  91 us
    reduce_scatter x1, waiting for transfers between devices, local(): lax.psum_scatter(jnp.dot(hidden, w_down, preferred_element_type=jnp.float...  36.8 us
    gather x3, local copies, waits for them, and re-layouts, to_slots(): return values[slot_source].reshape((peers, slot_length) + values.shape[1:])  27.8 us
    gather x2, local copies, waits for them, and re-layouts, local(): input_rows = landed.reshape(peers * slot_length, features)[flat_index]  21.2 us
    all_to_all x1, waiting for transfers between devices, local(): lax.all_to_all(out_slots, 'req', split_axis=0, concat_axis=0, tiled=True)  20.9 us
    dot_general x1, matrix products, local(): jnp.dot(hidden, w_down, preferred_element_type=jnp.float32)  11.4 us
  transfers between devices with their start and end apart: 5, of which 4 were waited for; matrix products, arithmetic and copies ran while one was open for 3% of the time, Pallas kernels for 0%

commit v1 on v0

--- a/solution.py
+++ b/solution.py
@@ -84,7 +84,19 @@
     tail_offset = wanted - block_id * block_len
     trailing = prefix_cache.shape[2:]
     initial = jnp.zeros((attach_slots.shape[0], window) + trailing, jnp.bfloat16)
-    shard_rows = lax.all_gather(prefix_cache, "req", axis=0, tiled=True)
+    how_many = lax.psum(1, "req")
+    parts_seen = [(jj, (jj + 1) % how_many) for jj in range(how_many)]
+    reached, odd = ([prefix_cache], [prefix_cache])
+    history = [(jj, (jj - 1) % how_many) for jj in range(how_many)]
+    for _ in range(how_many // 2):
+        reached.append(lax.ppermute(reached[-1], "req", parts_seen))
+    for _ in range((how_many - 1) // 2):
+        odd.append(lax.ppermute(odd[-1], axis_name="req", perm=history))
+    shard_rows = jnp.roll(
+        jnp.concatenate([*reached[::-1], *odd[1:]], axis=0),
+        (lax.axis_index("req") - how_many // 2) * prefix_cache.shape[0],
+        axis=0,
+    )
     held_blocks = shard_rows.shape[0]
     flat_rows = shard_rows.reshape((held_blocks * block_len,) + trailing)
     inside = (tail_store >= 0) & (tail_store < held_blocks)

time: 540 us -> 568 us (1.052)
  starting transfers between devices: 15 us -> 70 us
  waiting for transfers between devices: 326 us -> 287 us
  local copies, waits for them, and re-layouts: 103 us -> 112 us
    all_gather x1 -> x0, waiting for transfers between devices: 176 us -> none  [fetch_prefix(): shard_rows = lax.all_gather(prefix_cache, 'req', axis=0, tiled=True)]
    ppermute x0 -> x15, waiting for transfers between devices: none -> 140 us  [the longest x8 134 us: fetch_prefix(): reached.append(lax.ppermute(reached[-1], 'req', parts_seen))]
    ppermute x0 -> x15, starting transfers between devices: none -> 55.2 us  [the longest x7 44.5 us: fetch_prefix(): odd.append(lax.ppermute(odd[-1], axis_name='req', perm=history))]
    unnamed x28 -> x83, local copies, waits for them, and re-layouts: 9.1 us -> 27.7 us
    gather x3, local copies, waits for them, and re-layouts: 27.8 us -> 16.3 us  [to_slots(): return values[slot_source].reshape((peers, slot_length) + values.shape[1:])]
  transfers between devices with their start and end apart: 5 -> 19, of which waited for: 4 -> 14; matrix products, arithmetic and copies ran while one was open for 3% -> 7% of each run, Pallas kernels for 0% -> 0%
where the time goes in v1:
time: 568 us; the launch traced here: 559 us
  waiting for transfers between devices  287 us (51%)
  local copies, waits for them, and re-layouts  112 us (20%)
  starting transfers between devices  70 us (12%)
  matrix products  40.7 us (7%)
  other arithmetic  35.1 us (6%)
  between operations  14.2 us (2%)
    ppermute x8, waiting for transfers between devices, fetch_prefix(): reached.append(lax.ppermute(reached[-1], 'req', parts_seen))  134 us
    psum x1, waiting for transfers between devices, local(): lax.psum(partial_value.astype(jnp.bfloat16), 'tp').astype(jnp.float32)  89.6 us
    ppermute x7, starting transfers between devices, fetch_prefix(): odd.append(lax.ppermute(odd[-1], axis_name='req', perm=history))  44.5 us
    reduce_scatter x1, waiting for transfers between devices, local(): lax.psum_scatter(jnp.dot(hidden, w_down, preferred_element_type=jnp.float...  36.9 us
    unnamed x83, local copies, waits for them, and re-layouts  27.7 us
    gather x2, local copies, waits for them, and re-layouts, local(): input_rows = landed.reshape(peers * slot_length, features)[flat_index]  21.2 us
    all_to_all x1, waiting for transfers between devices, local(): lax.all_to_all(out_slots, 'req', split_axis=0, concat_axis=0, tiled=True)  20.8 us
    gather x3, local copies, waits for them, and re-layouts, to_slots(): return values[slot_source].reshape((peers, slot_length) + values.shape[1:])  16.3 us
  transfers between devices with their start and end apart: 19, of which 14 were waited for; matrix products, arithmetic and copies ran while one was open for 7% of the time, Pallas kernels for 0%

profile of v1, /device:TPU:7, one launch (start us, length us, event | category | flops | bytes accessed | tf_op | source)
XLA Modules:
  0.0 559.3 jit_solution(17251441327597955503)
XLA Ops:
  7.5 9.7 %gather_fusion = bf16[16,112,2880]{2,1,0:T(8,128)(2,1)} fusion(bf16[16,112,2880]{2,1,0:T(8,128)(2,1)} %param.15, s32[1024]{0:T(1024)S(1)} %pad_clamp_fusion.3), kind=kCustom, calls=%fused_computation | custom fusion | bytes 20643904 | tf_op jit(solution)/shard_map/gather | solution.py:158
  17.2 8.0 %all-to-all-start = ((bf16[16,112,2880]{2,1,0:T(8,128)(2,1)}), bf16[16,112,2880]{2,1,0:T(8,128)(2,1)}, u32[]{:S(2)}, u32[]{:S(2)}) async-start(bf16[16,112,2880]{2,1,0:T(8,128)(2,1)} %gather_fusion), calls=%async_computation | async-start | bytes 21102592 | tf_op jit(solution)/shard_map/all_to_all | solution.py:157
  35.4 118.0 %collective-permute-done = bf16[4,128,1,128]{3,1,2,0:T(8,128)(2,1)S(1)} collective-permute-done((bf16[4,128,1,128]{3,1,2,0:T(8,128)(2,1)S(1)}, bf16[4,128,1,128]{3,1,2,0:T(8,128)(2,1)S(1)}, u32[]{:S(2)}, u32[]{:S(2)}) %collective-permute-start) | collective-permute-done | bytes 131104 | tf_op jit(solution)/shard_map/ppermute | solution.py:92
  153.4 7.1 %collective-permute-done.1 = bf16[4,128,1,128]{3,1,2,0:T(8,128)(2,1)S(1)} collective-permute-done((bf16[4,128,1,128]{3,1,2,0:T(8,128)(2,1)S(1)}, bf16[4,128,1,128]{3,1,2,0:T(8,128)(2,1)S(1)}, u32[]{:S(2)}, u32[]{:S(2)}) %collective-permute-start.1) | collective-permute-done | bytes 131104 | tf_op jit(solution)/shard_map/ppermute | solution.py:92
  161.7 7.8 %collective-permute-start.9 = (bf16[4,128,1,128]{3,1,2,0:T(8,128)(2,1)S(1)}, bf16[4,128,1,128]{3,1,2,0:T(8,128)(2,1)}, u32[]{:S(2)}, u32[]{:S(2)}) collective-permute-start(bf16[4,128,1,128]{3,1,2,0:T(8,128)(2,1)S(1)} %collective-permute-done.8), channel_id=1, source_target_pairs={{0,120},{8,0},{16,8},{24,16},{32,24},{40,32},{48,40},{56,48},{64,5... | collective-permute-start | bytes 393224 | tf_op jit(solution)/shard_map/ppermute | solution.py:94
  171.4 6.7 %collective-permute-start.10 = (bf16[4,128,1,128]{3,1,2,0:T(8,128)(2,1)}, bf16[4,128,1,128]{3,1,2,0:T(8,128)(2,1)S(1)}, u32[]{:S(2)}, u32[]{:S(2)}) collective-permute-start(bf16[4,128,1,128]{3,1,2,0:T(8,128)(2,1)} %collective-permute-done.9), channel_id=1, source_target_pairs={{0,120},{8,0},{16,8},{24,16},{32,24},{40,32},{48,40},{56,48},{64,5... | collective-permute-start | bytes 393224 | tf_op jit(solution)/shard_map/ppermute | solution.py:94
  178.1 7.3 %collective-permute-done.3 = bf16[4,128,1,128]{3,1,2,0:T(8,128)(2,1)} collective-permute-done((bf16[4,128,1,128]{3,1,2,0:T(8,128)(2,1)}, bf16[4,128,1,128]{3,1,2,0:T(8,128)(2,1)}, u32[]{:S(2)}, u32[]{:S(2)}) %collective-permute-start.3) | collective-permute-done | bytes 131104 | tf_op jit(solution)/shard_map/ppermute | solution.py:92
  192.8 6.9 %collective-permute-start.5 = (bf16[4,128,1,128]{3,1,2,0:T(8,128)(2,1)S(1)}, bf16[4,128,1,128]{3,1,2,0:T(8,128)(2,1)S(1)}, u32[]{:S(2)}, u32[]{:S(2)}) collective-permute-start(bf16[4,128,1,128]{3,1,2,0:T(8,128)(2,1)S(1)} %collective-permute-done.4), channel_id=1, source_target_pairs={{0,8},{8,16},{16,24},{24,32},{32,40},{40,48},{48,56},{56,64},{64,7... | collective-permute-start | bytes 393224 | tf_op jit(solution)/shard_map/ppermute | solution.py:92
  201.0 12.5 %collective-permute-start.12 = (bf16[4,128,1,128]{3,1,2,0:T(8,128)(2,1)S(1)}, bf16[4,128,1,128]{3,1,2,0:T(8,128)(2,1)}, u32[]{:S(2)}, u32[]{:S(2)}) collective-permute-start(bf16[4,128,1,128]{3,1,2,0:T(8,128)(2,1)S(1)} %collective-permute-done.11), channel_id=1, source_target_pairs={{0,120},{8,0},{16,8},{24,16},{32,24},{40,32},{48,40},{56,48},{64,5... | collective-permute-start | bytes 393224 | tf_op jit(solution)/shard_map/ppermute | solution.py:94
  215.5 5.7 %collective-permute-start.13 = (bf16[4,128,1,128]{3,1,2,0:T(8,128)(2,1)}, bf16[4,128,1,128]{3,1,2,0:T(8,128)(2,1)}, u32[]{:S(2)}, u32[]{:S(2)}) collective-permute-start(bf16[4,128,1,128]{3,1,2,0:T(8,128)(2,1)} %collective-permute-done.12), channel_id=1, source_target_pairs={{0,120},{8,0},{16,8},{24,16},{32,24},{40,32},{48,40},{56,48},{64,5... | collective-permute-start | bytes 393224 | tf_op jit(solution)/shard_map/ppermute | solution.py:94
  223.4 6.1 %collective-permute-start.14 = (bf16[4,128,1,128]{3,1,2,0:T(8,128)(2,1)}, bf16[4,128,1,128]{3,1,2,0:T(8,128)(2,1)S(1)}, u32[]{:S(2)}, u32[]{:S(2)}) collective-permute-start(bf16[4,128,1,128]{3,1,2,0:T(8,128)(2,1)} %collective-permute-done.13), channel_id=1, source_target_pairs={{0,120},{8,0},{16,8},{24,16},{32,24},{40,32},{48,40},{56,48},{64,5... | collective-permute-start | bytes 393224 | tf_op jit(solution)/shard_map/ppermute | solution.py:94
  248.5 7.9 %gather_fusion.2 = bf16[2048,128]{1,0:T(8,128)(2,1)S(1)} fusion(bf16[8192,128]{1,0:T(8,128)(2,1)} %bitcast.89, s32[2048]{0:T(1024)S(1)} %get-tuple-element.19), kind=kCustom, calls=%fused_computation.2 | custom fusion | bytes 1056768 | tf_op jit(solution)/shard_map/gather | solution.py:103
  259.3 14.6 %gather_fusion.1 = bf16[768,2880]{1,0:T(8,128)(2,1)} fusion(bf16[1792,2880]{1,0:T(8,128)(2,1)} %bitcast.4, s32[1024]{0:T(1024)S(1)} %pad_clamp_fusion.2), kind=kCustom, calls=%fused_computation.1 | custom fusion | bytes 8850432 | tf_op jit(solution)/shard_map/gather | solution.py:160
  274.0 6.6 %copy.33 = bf16[768,2880]{0,1:T(8,128)(2,1)} copy(bf16[768,2880]{1,0:T(8,128)(2,1)} %gather_fusion.1) | data formatting | bytes 8847360 | tf_op jit(solution)/shard_map/gather | solution.py:160
  287.5 4.6 gather_fusion.3
  294.1 6.1 %fusion.20 = f32[768,512]{0,1:T(8,128)S(1)} fusion(bf16[2880,512]{1,0:T(8,128)(2,1)} %param.23, bf16[768,2880]{0,1:T(8,128)(2,1)} %copy.33, f32[2880]{0:T(1024)S(1)} %copy-done.15, f32[768]{0:T(1024)S(1)} %add_rsqrt_fusion.1), kind=kOutput, calls=%fused_computation.40 | convolution fusion | flops 2273771520 | bytes 8960256 | tf_op jit(solution)/shard_map/dot_general | solution.py:163
  308.1 3.7 subtract_convert_fusion
  313.9 5.7 %gather_fusion.4 = bf16[1792,8,64]{2,1,0:T(8,128)(2,1)} fusion(bf16[768,8,64]{2,1,0:T(8,128)(2,1)} %pad_maximum_fusion, s32[2048]{0:T(1024)S(1)} %get-tuple-element.20), kind=kCustom, calls=%fused_computation.4 | custom fusion | bytes 3677184 | tf_op jit(solution)/shard_map/gather | solution.py:154
  319.6 5.1 fusion.1
  324.8 5.3 fusion
  330.2 6.6 %convert_bitcast_fusion = bf16[16,112,1,8,64]{1,4,3,0,2:T(8,128)(2,1)} fusion(f32[16,8,112]{2,1,0:T(8,128)S(1)} %exponential_add_fusion, f32[16,8,112]{2,1,0:T(8,128)S(1)} %broadcast_maximum_fusion, f32[16,240,112,8]{1,2,3,0:T(8,128)S(1)} %get-tuple-element.18, pred[112,240]{1,0:T(8,128)(4,1)S(1)} %fusion.41, bf16[16,128,1,128]{1,3,0,2:T(8,128)(2,1)S(1)} %copy-done.3, ...), kind=kOutput, calls=%fused_computation.34 | convolution fusion | flops 459505664 | bytes 16722176 | tf_op jit(solution)/shard_map/nkgts,nskd->ntkgd/dot_general | solution.py:63
  336.8 4.8 copy.48
  341.6 5.9 %reshape.650 = bf16[1792,512]{1,0:T(8,128)(2,1)} reshape(bf16[16,112,1,8,64]{4,3,1,0,2:T(8,128)(2,1)} %copy.48) | data formatting | bytes 3670016 | tf_op jit(solution)/shard_map/reshape | solution.py:69
  347.5 5.3 gather_fusion.5
  352.8 5.7 %convolution_convert_fusion = bf16[768,2880]{0,1:T(8,128)(2,1)} fusion(bf16[768,512]{1,0:T(8,128)(2,1)} %gather_fusion.5, bf16[512,2880]{0,1:T(8,128)(2,1)S(1)} %copy-done), kind=kOutput, calls=%fused_computation.28 | convolution fusion | flops 2267136000 | bytes 8159232 | tf_op jit(solution)/shard_map/dot_general | solution.py:173
  359.2 89.6 %all-reduce.2.cloned.1.call-done = bf16[768,2880]{0,1:T(8,128)(2,1)} async-done(((bf16[768,2880]{0,1:T(8,128)(2,1)}), bf16[768,2880]{0,1:T(8,128)(2,1)}) %all-reduce.2.cloned.1.call-update) | async-done | bytes 4423696 | tf_op jit(solution)/shard_map/psum | solution.py:174
  448.8 5.5 fusion.2
  459.6 11.3 %convolution_convert_fusion.1 = bf16[768,2880]{0,1:T(8,128)(2,1)} fusion(bf16[360,2880]{1,0:T(8,128)(2,1)} %param.29, bf16[2880,360]{0,1:T(8,128)(2,1)} %param.28, bf16[768,2880]{0,1:T(8,128)(2,1)} %copy-done.2, f32[2880]{0:T(1024)S(1)} %convert_element_type.103, f32[768]{0:T(1024)S(1)} %add_rsqrt_fusion, f32[768,360]{0,1:T(8,128)} %fusion.18), kind=kOutput, calls=%fused_computation.29 | convolution fusion | flops 3197767680 | bytes 14115072 | tf_op jit(solution)/shard_map/dot_general | solution.py:184
  471.7 36.9 %reduce-scatter.2.cloned.1.call-done = bf16[768,360]{0,1:T(8,128)(2,1)} async-done(((bf16[768,2880]{0,1:T(8,128)(2,1)}), bf16[768,360]{0,1:T(8,128)(2,1)}) %reduce-scatter.2.cloned.1.call-update) | async-done | bytes 552976 | tf_op jit(solution)/shard_map/reduce_scatter | solution.py:183
  512.1 6.0 %gather_fusion.6 = bf16[1792,360]{1,0:T(8,128)(2,1)} fusion(bf16[768,360]{1,0:T(8,128)(2,1)S(1)} %copy.43, s32[2048]{0:T(1024)S(1)} %get-tuple-element.20), kind=kCustom, calls=%fused_computation.6 | custom fusion | bytes 2587648 | tf_op jit(solution)/shard_map/gather | solution.py:154
  520.8 6.7 %all-to-all-start.1 = ((bf16[16,112,360]{2,1,0:T(8,128)(2,1)}), bf16[16,112,360]{2,1,0:T(8,128)(2,1)}, u32[]{:S(2)}, u32[]{:S(2)}) async-start(bf16[16,112,360]{2,1,0:T(8,128)(2,1)} %broadcast_select_fusion), calls=%async_computation.2 | async-start | bytes 2752512 | tf_op jit(solution)/shard_map/all_to_all | solution.py:191
  528.2 20.8 %all-to-all-done.1 = bf16[16,112,360]{2,1,0:T(8,128)(2,1)} async-done(((bf16[16,112,360]{2,1,0:T(8,128)(2,1)}), bf16[16,112,360]{2,1,0:T(8,128)(2,1)}, u32[]{:S(2)}, u32[]{:S(2)}) %all-to-all-start.1) | async-done | bytes 1290272 | tf_op jit(solution)/shard_map/all_to_all | solution.py:191
  (169 shorter events, 84.8 us)
Async XLA Ops:
  6.5 346.3 %copy-start = (bf16[512,2880]{0,1:T(8,128)(2,1)S(1)}, bf16[512,2880]{0,1:T(8,128)(2,1)}, u32[]{:S(2)}) copy-start(bf16[512,2880]{0,1:T(8,128)(2,1)} %param.25) | copy-start | bytes 8847364
  17.2 8.0 %copy-start.6 = (bf16[4,128,1,128]{3,1,2,0:T(8,128)(2,1)S(1)}, bf16[4,128,1,128]{3,1,2,0:T(8,128)(2,1)}, u32[]{:S(2)}) copy-start(bf16[4,128,1,128]{3,1,2,0:T(8,128)(2,1)} %param.19) | copy-start | bytes 393220
  17.2 13.8 %copy-start.23 = (s32[256]{0:T(256)S(1)}, s32[256]{0:T(256)}, u32[]{:S(2)}) copy-start(s32[256]{0:T(256)} %param.18) | copy-start | bytes 3076
  17.2 13.9 %copy-start.16 = (s32[16,16]{1,0:T(8,128)S(1)}, s32[16,16]{1,0:T(8,128)}, u32[]{:S(2)}) copy-start(s32[16,16]{1,0:T(8,128)} %param.17) | copy-start | bytes 3076
  17.2 204.5 %copy-start.17 = (bf16[2880]{0:T(1024)(128)(2,1)S(1)}, bf16[2880]{0:T(1024)(128)(2,1)}, u32[]{:S(2)}) copy-start(bf16[2880]{0:T(1024)(128)(2,1)} %param.22) | copy-start | bytes 17284
  17.2 242.2 %all-to-all-start = ((bf16[16,112,2880]{2,1,0:T(8,128)(2,1)}), bf16[16,112,2880]{2,1,0:T(8,128)(2,1)}, u32[]{:S(2)}, u32[]{:S(2)}) async-start(bf16[16,112,2880]{2,1,0:T(8,128)(2,1)} %gather_fusion), calls=%async_computation | async-start | bytes 21102592 | tf_op jit(solution)/shard_map/all_to_all | solution.py:157
  25.1 423.7 %all-reduce.2.cloned.1.call-start = ((), (), s32[]{:S(2)}) async-start(), calls=%async_computation.3 | async-start | bytes 8847360 | tf_op jit(solution)/shard_map/psum | solution.py:174
  25.2 128.2 %collective-permute-start = (bf16[4,128,1,128]{3,1,2,0:T(8,128)(2,1)S(1)}, bf16[4,128,1,128]{3,1,2,0:T(8,128)(2,1)S(1)}, u32[]{:S(2)}, u32[]{:S(2)}) collective-permute-start(bf16[4,128,1,128]{3,1,2,0:T(8,128)(2,1)S(1)} %copy-done.6), channel_id=1, source_target_pairs={{0,8},{8,16},{16,24},{24,32},{32,40},{40,48},{48,56},{56,64},{64,7... | collective-permute-start | bytes 393224 | tf_op jit(solution)/shard_map/ppermute | solution.py:92
  26.6 135.1 %collective-permute-start.8 = (bf16[4,128,1,128]{3,1,2,0:T(8,128)(2,1)S(1)}, bf16[4,128,1,128]{3,1,2,0:T(8,128)(2,1)S(1)}, u32[]{:S(2)}, u32[]{:S(2)}) collective-permute-start(bf16[4,128,1,128]{3,1,2,0:T(8,128)(2,1)S(1)} %copy-done.6), channel_id=1, source_target_pairs={{0,120},{8,0},{16,8},{24,16},{32,24},{40,32},{48,40},{56,48},{64,5... | collective-permute-start | bytes 393224 | tf_op jit(solution)/shard_map/ppermute | solution.py:94
  31.1 122.3 %copy-start.21 = (f32[32]{0:T(128)}, f32[32]{0:T(128)S(1)}, u32[]{:S(2)}) copy-start(f32[32]{0:T(128)S(1)} %negate_power_fusion) | copy-start | bytes 388
  153.4 7.1 %collective-permute-start.1 = (bf16[4,128,1,128]{3,1,2,0:T(8,128)(2,1)S(1)}, bf16[4,128,1,128]{3,1,2,0:T(8,128)(2,1)S(1)}, u32[]{:S(2)}, u32[]{:S(2)}) collective-permute-start(bf16[4,128,1,128]{3,1,2,0:T(8,128)(2,1)S(1)} %collective-permute-done), channel_id=1, source_target_pairs={{0,8},{8,16},{16,24},{24,32},{32,40},{40,48},{48,56},{56,64},{64,7... | collective-permute-start | bytes 393224 | tf_op jit(solution)/shard_map/ppermute | solution.py:92
  160.5 9.0 %collective-permute-start.2 = (bf16[4,128,1,128]{3,1,2,0:T(8,128)(2,1)S(1)}, bf16[4,128,1,128]{3,1,2,0:T(8,128)(2,1)}, u32[]{:S(2)}, u32[]{:S(2)}) collective-permute-start(bf16[4,128,1,128]{3,1,2,0:T(8,128)(2,1)S(1)} %collective-permute-done.1), channel_id=1, source_target_pairs={{0,8},{8,16},{16,24},{24,32},{32,40},{40,48},{48,56},{56,64},{64,7... | collective-permute-start | bytes 393224 | tf_op jit(solution)/shard_map/ppermute | solution.py:92
  160.5 9.1 %copy-start.20 = (s32[16]{0:T(128)}, s32[16]{0:T(128)S(1)}, u32[]{:S(2)}) copy-start(s32[16]{0:T(128)S(1)} %broadcast_add_fusion) | copy-start | bytes 196
  161.7 9.8 %collective-permute-start.9 = (bf16[4,128,1,128]{3,1,2,0:T(8,128)(2,1)S(1)}, bf16[4,128,1,128]{3,1,2,0:T(8,128)(2,1)}, u32[]{:S(2)}, u32[]{:S(2)}) collective-permute-start(bf16[4,128,1,128]{3,1,2,0:T(8,128)(2,1)S(1)} %collective-permute-done.8), channel_id=1, source_target_pairs={{0,120},{8,0},{16,8},{24,16},{32,24},{40,32},{48,40},{56,48},{64,5... | collective-permute-start | bytes 393224 | tf_op jit(solution)/shard_map/ppermute | solution.py:94
  169.5 15.9 %collective-permute-start.3 = (bf16[4,128,1,128]{3,1,2,0:T(8,128)(2,1)}, bf16[4,128,1,128]{3,1,2,0:T(8,128)(2,1)}, u32[]{:S(2)}, u32[]{:S(2)}) collective-permute-start(bf16[4,128,1,128]{3,1,2,0:T(8,128)(2,1)} %collective-permute-done.2), channel_id=1, source_target_pairs={{0,8},{8,16},{16,24},{24,32},{32,40},{40,48},{48,56},{56,64},{64,7... | collective-permute-start | bytes 393224 | tf_op jit(solution)/shard_map/ppermute | solution.py:92
  171.4 17.4 %collective-permute-start.10 = (bf16[4,128,1,128]{3,1,2,0:T(8,128)(2,1)}, bf16[4,128,1,128]{3,1,2,0:T(8,128)(2,1)S(1)}, u32[]{:S(2)}, u32[]{:S(2)}) collective-permute-start(bf16[4,128,1,128]{3,1,2,0:T(8,128)(2,1)} %collective-permute-done.9), channel_id=1, source_target_pairs={{0,120},{8,0},{16,8},{24,16},{32,24},{40,32},{48,40},{56,48},{64,5... | collective-permute-start | bytes 393224 | tf_op jit(solution)/shard_map/ppermute | solution.py:94
  185.4 7.3 %collective-permute-start.4 = (bf16[4,128,1,128]{3,1,2,0:T(8,128)(2,1)}, bf16[4,128,1,128]{3,1,2,0:T(8,128)(2,1)S(1)}, u32[]{:S(2)}, u32[]{:S(2)}) collective-permute-start(bf16[4,128,1,128]{3,1,2,0:T(8,128)(2,1)} %collective-permute-done.3), channel_id=1, source_target_pairs={{0,8},{8,16},{16,24},{24,32},{32,40},{40,48},{48,56},{56,64},{64,7... | collective-permute-start | bytes 393224 | tf_op jit(solution)/shard_map/ppermute | solution.py:92
  189.5 10.9 %collective-permute-start.11 = (bf16[4,128,1,128]{3,1,2,0:T(8,128)(2,1)S(1)}, bf16[4,128,1,128]{3,1,2,0:T(8,128)(2,1)S(1)}, u32[]{:S(2)}, u32[]{:S(2)}) collective-permute-start(bf16[4,128,1,128]{3,1,2,0:T(8,128)(2,1)S(1)} %collective-permute-done.10), channel_id=1, source_target_pairs={{0,120},{8,0},{16,8},{24,16},{32,24},{40,32},{48,40},{56,48},{64,5... | collective-permute-start | bytes 393224 | tf_op jit(solution)/shard_map/ppermute | solution.py:94
  192.8 22.7 %copy-start.11 = (bf16[4,128,1,128]{3,1,2,0:T(8,128)(2,1)}, bf16[4,128,1,128]{3,1,2,0:T(8,128)(2,1)S(1)}, u32[]{:S(2)}) copy-start(bf16[4,128,1,128]{3,1,2,0:T(8,128)(2,1)S(1)} %collective-permute-done.4) | copy-start | bytes 393220
  192.8 20.9 %collective-permute-start.5 = (bf16[4,128,1,128]{3,1,2,0:T(8,128)(2,1)S(1)}, bf16[4,128,1,128]{3,1,2,0:T(8,128)(2,1)S(1)}, u32[]{:S(2)}, u32[]{:S(2)}) collective-permute-start(bf16[4,128,1,128]{3,1,2,0:T(8,128)(2,1)S(1)} %collective-permute-done.4), channel_id=1, source_target_pairs={{0,8},{8,16},{16,24},{24,32},{32,40},{40,48},{48,56},{56,64},{64,7... | collective-permute-start | bytes 393224 | tf_op jit(solution)/shard_map/ppermute | solution.py:92
  201.0 14.5 %collective-permute-start.12 = (bf16[4,128,1,128]{3,1,2,0:T(8,128)(2,1)S(1)}, bf16[4,128,1,128]{3,1,2,0:T(8,128)(2,1)}, u32[]{:S(2)}, u32[]{:S(2)}) collective-permute-start(bf16[4,128,1,128]{3,1,2,0:T(8,128)(2,1)S(1)} %collective-permute-done.11), channel_id=1, source_target_pairs={{0,120},{8,0},{16,8},{24,16},{32,24},{40,32},{48,40},{56,48},{64,5... | collective-permute-start | bytes 393224 | tf_op jit(solution)/shard_map/ppermute | solution.py:94
  213.7 8.0 %collective-permute-start.6 = (bf16[4,128,1,128]{3,1,2,0:T(8,128)(2,1)S(1)}, bf16[4,128,1,128]{3,1,2,0:T(8,128)(2,1)}, u32[]{:S(2)}, u32[]{:S(2)}) collective-permute-start(bf16[4,128,1,128]{3,1,2,0:T(8,128)(2,1)S(1)} %collective-permute-done.5), channel_id=1, source_target_pairs={{0,8},{8,16},{16,24},{24,32},{32,40},{40,48},{48,56},{56,64},{64,7... | collective-permute-start | bytes 393224 | tf_op jit(solution)/shard_map/ppermute | solution.py:92
  215.5 7.9 %collective-permute-start.13 = (bf16[4,128,1,128]{3,1,2,0:T(8,128)(2,1)}, bf16[4,128,1,128]{3,1,2,0:T(8,128)(2,1)}, u32[]{:S(2)}, u32[]{:S(2)}) collective-permute-start(bf16[4,128,1,128]{3,1,2,0:T(8,128)(2,1)} %collective-permute-done.12), channel_id=1, source_target_pairs={{0,120},{8,0},{16,8},{24,16},{32,24},{40,32},{48,40},{56,48},{64,5... | collective-permute-start | bytes 393224 | tf_op jit(solution)/shard_map/ppermute | solution.py:94
  221.7 8.3 %collective-permute-start.7 = (bf16[4,128,1,128]{3,1,2,0:T(8,128)(2,1)}, bf16[4,128,1,128]{3,1,2,0:T(8,128)(2,1)}, u32[]{:S(2)}, u32[]{:S(2)}) collective-permute-start(bf16[4,128,1,128]{3,1,2,0:T(8,128)(2,1)} %collective-permute-done.6), channel_id=1, source_target_pairs={{0,8},{8,16},{16,24},{24,32},{32,40},{40,48},{48,56},{56,64},{64,7... | collective-permute-start | bytes 393224 | tf_op jit(solution)/shard_map/ppermute | solution.py:92
  222.3 19.9 %copy-start.14 = (bf16[4,128,1,128]{3,1,2,0:T(8,128)(2,1)S(1)}, bf16[4,128,1,128]{3,1,2,0:T(8,128)(2,1)}, u32[]{:S(2)}) copy-start(bf16[4,128,1,128]{3,1,2,0:T(8,128)(2,1)} %copy-done.13) | copy-start | bytes 393220
  222.3 19.9 %copy-start.12 = (bf16[4,128,1,128]{3,1,2,0:T(8,128)(2,1)S(1)}, bf16[4,128,1,128]{3,1,2,0:T(8,128)(2,1)}, u32[]{:S(2)}) copy-start(bf16[4,128,1,128]{3,1,2,0:T(8,128)(2,1)} %copy-done.11) | copy-start | bytes 393220
  222.3 22.8 %copy-start.8 = (bf16[4,128,1,128]{3,1,2,0:T(8,128)(2,1)S(1)}, bf16[4,128,1,128]{3,1,2,0:T(8,128)(2,1)}, u32[]{:S(2)}) copy-start(bf16[4,128,1,128]{3,1,2,0:T(8,128)(2,1)} %copy-done.7) | copy-start | bytes 393220
  222.3 22.9 %copy-start.10 = (bf16[4,128,1,128]{3,1,2,0:T(8,128)(2,1)S(1)}, bf16[4,128,1,128]{3,1,2,0:T(8,128)(2,1)}, u32[]{:S(2)}) copy-start(bf16[4,128,1,128]{3,1,2,0:T(8,128)(2,1)} %copy-done.9) | copy-start | bytes 393220
  223.4 16.8 %collective-permute-start.14 = (bf16[4,128,1,128]{3,1,2,0:T(8,128)(2,1)}, bf16[4,128,1,128]{3,1,2,0:T(8,128)(2,1)S(1)}, u32[]{:S(2)}, u32[]{:S(2)}) collective-permute-start(bf16[4,128,1,128]{3,1,2,0:T(8,128)(2,1)} %collective-permute-done.13), channel_id=1, source_target_pairs={{0,120},{8,0},{16,8},{24,16},{32,24},{40,32},{48,40},{56,48},{64,5... | collective-permute-start | bytes 393224 | tf_op jit(solution)/shard_map/ppermute | solution.py:94
  358.6 150.0 %reduce-scatter.2.cloned.1.call-start = ((), (), s32[]{:S(2)}) async-start(), calls=%async_computation.4 | async-start | bytes 4976640 | tf_op jit(solution)/shard_map/reduce_scatter | solution.py:183
  448.8 7.5 %copy-start.24 = (bf16[2880,360]{0,1:T(8,128)(2,1)S(1)}, bf16[2880,360]{0,1:T(8,128)(2,1)}, u32[]{:S(2)}) copy-start(bf16[2880,360]{0,1:T(8,128)(2,1)} %param.27) | copy-start | bytes 6220804
  520.8 28.2 %all-to-all-start.1 = ((bf16[16,112,360]{2,1,0:T(8,128)(2,1)}), bf16[16,112,360]{2,1,0:T(8,128)(2,1)}, u32[]{:S(2)}, u32[]{:S(2)}) async-start(bf16[16,112,360]{2,1,0:T(8,128)(2,1)} %broadcast_select_fusion), calls=%async_computation.2 | async-start | bytes 2752512 | tf_op jit(solution)/shard_map/all_to_all | solution.py:191
  (12 other events, 44.1 us)
Sparse Core Ops, SparseCore 0:
  358.7 90.0 all-reduce.1
  471.1 37.4 reduce-scatter.1
